TPU v7x, 32 devices: a whole 2x2x4 slice. The times are simulated.
32 devices in a mesh: clips: 2 (over x), rows: 16 (over z, y, core).
Axes of the slice: x: 2, y: 2, z: 4, core: 2. Of those that a mesh axis runs over, the one named last changes fastest.
Arguments:
- frames: bfloat16 [2, 32, 128, 384], P('clips', 'rows'), parts along dimension 0, may hold values from -48 to 48
- norm_attn: float32 [384], replicated, may hold values from 0.25 to 1.75
- w_query: bfloat16 [384, 384], replicated, may hold values from -12 to 12
- w_key: bfloat16 [384, 384], replicated, may hold values from -12 to 12
- w_value: bfloat16 [384, 384], replicated, may hold values from -2 to 2
- w_out: bfloat16 [384, 384], replicated, may hold values from -9 to 9
- cache_one: bfloat16 [4, 32, 128, 384], P('clips', 'rows'), parts along dimension 0, may hold values from -6 to 6
- norm_conv: float32 [384], replicated, may hold values from 0.25 to 1.75
- conv_weight: bfloat16 [3, 3, 3, 384, 384], replicated, may hold values from -0.109375 to 0.109375
- w_up: bfloat16 [3, 3, 384, 192], replicated, may hold values from -0.109375 to 0.109375
Outputs:
- upsampled: bfloat16 [2, 64, 49152], P('clips', 'rows'), parts along dimension 0
There are 2 independent parts, one for each index of `clips`. A program takes and returns all parts, laid end to end along the dimension named above; an argument that names none is the same for every part. Nothing has to cross between parts.
All inputs are finite; a program needn't handle non-finite values.
Results may differ from a plain program's by a relative error of at most 0.013.
Values may be sent and summed in bfloat16 or wider, within the bound.
No kernel may reach another device: no remote copies, remote signals or barrier semaphores. Data moves between devices by JAX's collectives and lax.ppermute only.
A program may use at most 128 MiB of HBM per device.

v0:
```python
import jax
import jax.numpy as jnp
from jax import lax
from jax.sharding import PartitionSpec as P

EPS = 1e-06


def padded_2(array, sides, width):
    for axis, dim in sides:
        size, length = (lax.axis_size(axis), array.shape[dim])
        up = [(i, (i + 1) % size) for i in range(size - 1)]
        down = [(j, i) for i, j in up]
        last = lax.slice_in_dim(array, length - width, length, axis=dim)
        first = lax.slice_in_dim(array, 0, width, axis=dim)
        before = lax.ppermute(last, axis, up)
        after = lax.ppermute(first, axis, down)
        array = jnp.concatenate([before, array, after], axis=dim)
    return array


def rms_gain(values, gain):
    return values * lax.rsqrt(jnp.mean(values * values, axis=-1, keepdims=True) + EPS) * gain


def project(inputs, weight):
    return jnp.einsum("fqc,cd->fqd", inputs, weight, preferred_element_type=jnp.float32).astype(
        jnp.bfloat16
    )


def conv_core(padded, weight, frames_out, rows_out, cols_out):
    chans = padded.shape[-1]
    outs = weight.shape[-1]
    wide = jnp.concatenate(
        [padded[:, :, shift : shift + cols_out, :] for shift in range(3)], axis=-1
    )
    total = jnp.zeros((frames_out * rows_out * cols_out, outs), jnp.float32)
    for tstep in range(weight.shape[0]):
        for rstep in range(3):
            part = wide[tstep : tstep + frames_out, rstep : rstep + rows_out].reshape(-1, 3 * chans)
            total = total + jnp.dot(
                part,
                weight[tstep, rstep].reshape(3 * chans, outs),
                preferred_element_type=jnp.float32,
            )
    return total


def attend_block(carry, queries, keys, values, scale):
    running, denom, accum = carry
    scores = jnp.einsum("fqc,fkc->fqk", queries, keys, preferred_element_type=jnp.float32) * scale
    newtop = jnp.maximum(running, jnp.max(scores, axis=-1))
    expo = jnp.exp(scores - newtop[..., None])
    denom = jnp.sum(expo, axis=-1)
    accum = jnp.einsum(
        "fqk,fkc->fqc", expo.astype(jnp.bfloat16), values, preferred_element_type=jnp.float32
    )
    return (newtop, denom, accum)


def body(
    frames, norm_attn, w_query, w_key, w_value, w_out, cache_one, norm_conv, conv_weight, w_up
):
    nframes, nrows, ncols, chans = frames.shape
    scale = chans ** (-0.5)
    flat = frames.reshape(nframes, nrows * ncols, chans)
    normed = rms_gain(flat.astype(jnp.float32), norm_attn).astype(jnp.bfloat16)
    queries = project(normed, w_query)
    start_carry = (
        jnp.full((nframes, nrows * ncols), -1e30, jnp.float32),
        jnp.zeros((nframes, nrows * ncols), jnp.float32),
        jnp.zeros((nframes, nrows * ncols, chans), jnp.float32),
    )
    keys = project(normed, w_key).reshape(nframes, nrows, ncols, chans)
    values = project(normed, w_value).reshape(nframes, nrows, ncols, chans)
    keys_in = lax.all_gather(keys, "rows", axis=1, tiled=True).reshape(nframes, -1, chans)
    values_in = lax.all_gather(values, "rows", axis=1, tiled=True).reshape(nframes, -1, chans)
    carry = attend_block(start_carry, queries, keys_in, values_in, scale)
    attended = (carry[2] / carry[1][..., None]).astype(jnp.bfloat16)
    mixed = (
        flat.astype(jnp.float32)
        + jnp.einsum("fqc,cd->fqd", attended, w_out, preferred_element_type=jnp.float32)
    ).astype(jnp.bfloat16)
    activ = (
        jax.nn.silu(rms_gain(mixed.astype(jnp.float32), norm_conv))
        .astype(jnp.bfloat16)
        .reshape(nframes, nrows, ncols, chans)
    )
    stack = jnp.concatenate([cache_one, activ], axis=0)
    haloed = padded_2(stack, (("rows", 1),), 1)
    padded = jnp.pad(haloed, ((0, 0), (0, 0), (1, 1), (0, 0)))
    conv_out = (
        conv_core(padded, conv_weight, nframes, nrows, ncols)
        .astype(jnp.bfloat16)
        .reshape(nframes, nrows, ncols, chans)
    )
    extended = padded_2(conv_out, (("rows", 1),), 1)
    doubled = jnp.repeat(jnp.repeat(extended, 2, axis=1), 2, axis=2)[:, 1 : 2 * nrows + 3]
    padded_up = jnp.pad(doubled, ((0, 0), (0, 0), (1, 1), (0, 0)))
    result = conv_core(padded_up, w_up[None], nframes, 2 * nrows, 2 * ncols)
    return result.astype(jnp.bfloat16).reshape(nframes, 2 * nrows, 2 * ncols * w_up.shape[-1])


def solution(mesh):
    placed = (
        P("clips", "rows", None, None),
        P(),
        P(),
        P(),
        P(),
        P(),
        P("clips", "rows", None, None),
        P(),
        P(),
        P(),
    )
    return jax.shard_map(
        body, mesh=mesh, in_specs=placed, out_specs=P("clips", "rows", None), check_vma=False
    )
```

profile of v0, /device:TPU:5, one launch (start us, length us, event | category | flops | bytes accessed | tf_op | source)
XLA Modules:
  0.0 151.7 jit_solution(1694360441257205537)
XLA Ops:
  6.5 1.1 multiply_reduce_fusion.1
  7.6 1.0 fusion.29
  8.7 1.9 %convolution_convert_fusion.1 = bf16[256,384]{1,0:T(8,128)(2,1)} fusion(bf16[256,384]{1,0:T(8,128)(2,1)S(1)} %fusion.29, bf16[384,384]{1,0:T(8,128)(2,1)} %param.13), kind=kOutput, calls=%fused_computation.30 | convolution fusion | flops 75595776 | bytes 688128 | tf_op jit(solution)/shard_map/fqc,cd->fqd/dot_general | solution.py:27
  10.7 1.9 %convolution_convert_fusion = bf16[256,384]{1,0:T(8,128)(2,1)} fusion(bf16[256,384]{1,0:T(8,128)(2,1)S(1)} %fusion.29, bf16[384,384]{1,0:T(8,128)(2,1)} %param.14), kind=kOutput, calls=%fused_computation.29 | convolution fusion | flops 75595776 | bytes 688128 | tf_op jit(solution)/shard_map/fqc,cd->fqd/dot_general | solution.py:27
  12.6 44.3 %all-gather.3.cloned.1.call-done = bf16[1,32,128,384]{3,2,0,1:T(8,128)(2,1)} async-done(((bf16[1,2,128,384]{3,2,0,1:T(8,128)(2,1)}), bf16[1,32,128,384]{3,2,0,1:T(8,128)(2,1)}) %all-gather.3.cloned.1.call-update) | async-done | bytes 3145744 | tf_op jit(solution)/shard_map/all_gather | solution.py:77
  56.9 5.3 %fusion.38 = (f32[256]{0:T(256)S(1)}, f32[256,4096]{1,0:T(8,128)}) fusion(bf16[4096,384]{1,0:T(8,128)(2,1)} %bitcast.108, bf16[256,384]{1,0:T(8,128)(2,1)S(1)} %fusion.29, bf16[384,384]{1,0:T(8,128)(2,1)S(1)} %copy-done), kind=kOutput, calls=%fused_computation.59 | convolution fusion | flops 882999040 | bytes 7832576 | tf_op jit(solution)/shard_map/fqc,fkc->fqk/dot_general | solution.py:52
  62.3 3.0 %fusion = f32[256]{0:T(256)S(1)} fusion(f32[256,4096]{1,0:T(8,128)} %get-tuple-element.38, f32[256]{0:T(256)S(1)} %broadcast_maximum_fusion), kind=kLoop, calls=%fused_computation.4 | loop fusion | flops 2096896 | bytes 4196352 | tf_op jit(solution)/shard_map/reduce_sum | solution.py:55
  65.2 37.8 %all-gather.5.cloned.1.call-done = bf16[1,32,128,384]{3,2,0,1:T(8,128)(2,1)} async-done(((bf16[1,2,128,384]{3,2,0,1:T(8,128)(2,1)}), bf16[1,32,128,384]{3,2,0,1:T(8,128)(2,1)}) %all-gather.5.cloned.1.call-update) | async-done | bytes 3145744 | tf_op jit(solution)/shard_map/all_gather | solution.py:78
  103.0 4.8 %multiply_reduce_fusion = (f32[256]{0:T(256)S(1)}, f32[256,384]{1,0:T(8,128)S(1)}) fusion(bf16[384,384]{1,0:T(8,128)(2,1)S(1)} %copy-done.9, bf16[4096,384]{1,0:T(8,128)(2,1)} %bitcast.130, f32[256,4096]{1,0:T(8,128)} %get-tuple-element.38, f32[256]{0:T(256)S(1)} %broadcast_maximum_fusion, f32[256]{0:T(256)S(1)} %fusion, bf16[256,384]{1,0:T(8,128)(2,1)S(1)} %bitcast.127), kind=kOutput, calls=%fused_computation.45 | convolution fusion | flops 883687168 | bytes 8227840 | tf_op jit(solution)/shard_map/fqc,cd->fqd/dot_general | solution.py:83
  107.9 0.2 multiply_convert_fusion
  108.2 4.1 %collective-permute-start = (bf16[3,1,128,384]{3,2,1,0:T(8,128)(2,1)S(1)}, bf16[3,1,128,384]{3,2,1,0:T(8,128)(2,1)S(1)}, u32[]{:S(2)}, u32[]{:S(2)}) collective-permute-start(bf16[3,1,128,384]{3,2,1,0:T(8,128)(2,1)S(1)} %get-tuple-element.33), channel_id=1, source_target_pairs={{0,1},{1,2},{2,3},{3,4},{4,5},{5,6},{6,7},{7,8},{8,9},{9,10},{10,1... | collective-permute-start | bytes 884744 | tf_op jit(solution)/shard_map/ppermute | solution.py:16
  112.3 1.9 %collective-permute-start.1 = (bf16[3,1,128,384]{3,2,1,0:T(8,128)(2,1)S(1)}, bf16[3,1,128,384]{3,2,1,0:T(8,128)(2,1)S(1)}, u32[]{:S(2)}, u32[]{:S(2)}) collective-permute-start(bf16[3,1,128,384]{3,2,1,0:T(8,128)(2,1)S(1)} %get-tuple-element.34), channel_id=1, source_target_pairs={{1,0},{2,1},{3,2},{4,3},{5,4},{6,5},{7,6},{8,7},{9,8},{10,9},{11,1... | collective-permute-start | bytes 884744 | tf_op jit(solution)/shard_map/ppermute | solution.py:17
  114.2 3.9 %fusion.32 = (bf16[1,1,3,384,384]{4,3,2,1,0:T(8,128)(2,1)S(1)}, bf16[1,1,3,384,384]{4,3,2,1,0:T(8,128)(2,1)S(1)}, bf16[1,1,3,384,384]{4,3,2,1,0:T(8,128)(2,1)S(1...) fusion(bf16[3,3,3,384,384]{4,3,2,1,0:T(8,128)(2,1)} %param.18), kind=kLoop, calls=%fused_computation.53 | loop fusion | bytes 15925248 | tf_op jit(solution)/shard_map/slice | solution.py:44
  118.2 3.1 %collective-permute-done.1 = bf16[3,1,128,384]{3,2,1,0:T(8,128)(2,1)S(1)} collective-permute-done((bf16[3,1,128,384]{3,2,1,0:T(8,128)(2,1)S(1)}, bf16[3,1,128,384]{3,2,1,0:T(8,128)(2,1)S(1)}, u32[]{:S(2)}, u32[]{:S(2)}) %collective-permute-start.1) | collective-permute-done | bytes 294944 | tf_op jit(solution)/shard_map/ppermute | solution.py:17
  121.2 0.3 select_maximum_fusion
  121.6 0.5 fusion.36
  122.1 0.5 pad_maximum_fusion
  122.7 0.7 fusion.34
  123.4 0.5 fusion.41
  123.9 0.5 fusion.42
  124.4 0.5 fusion.43
  124.8 0.5 fusion.44
  125.3 0.5 fusion.45
  125.8 0.5 fusion.46
  126.3 0.5 fusion.47
  126.8 0.5 fusion.48
  127.3 0.6 fusion.17
  127.9 1.9 %collective-permute-start.2 = (bf16[1,1,128,384]{3,2,1,0:T(8,128)(2,1)S(1)}, bf16[1,1,128,384]{3,2,1,0:T(8,128)(2,1)S(1)}, u32[]{:S(2)}, u32[]{:S(2)}) collective-permute-start(bf16[1,1,128,384]{3,2,1,0:T(8,128)(2,1)S(1)} %get-tuple-element.35), channel_id=1, source_target_pairs={{0,1},{1,2},{2,3},{3,4},{4,5},{5,6},{6,7},{7,8},{8,9},{9,10},{10,1... | collective-permute-start | bytes 294920 | tf_op jit(solution)/shard_map/ppermute | solution.py:16
  129.9 2.6 %collective-permute-start.3 = (bf16[1,1,128,384]{3,2,1,0:T(8,128)(2,1)S(1)}, bf16[1,1,128,384]{3,2,1,0:T(8,128)(2,1)S(1)}, u32[]{:S(2)}, u32[]{:S(2)}) collective-permute-start(bf16[1,1,128,384]{3,2,1,0:T(8,128)(2,1)S(1)} %get-tuple-element.36), channel_id=1, source_target_pairs={{1,0},{2,1},{3,2},{4,3},{5,4},{6,5},{7,6},{8,7},{9,8},{10,9},{11,1... | collective-permute-start | bytes 294920 | tf_op jit(solution)/shard_map/ppermute | solution.py:17
  132.5 0.1 fusion.35
  132.6 0.4 copy.17
  133.0 0.8 copy.21
  133.8 0.4 copy.18
  134.2 0.8 copy.22
  135.0 0.4 copy.19
  135.4 0.8 copy.23
  136.3 0.4 collective-permute-done.3
  136.8 0.8 broadcast_in_dim.25
  137.6 0.6 broadcast_in_dim.26
  138.3 0.1 slice.149
  138.4 0.5 pad_slice_fusion.1
  139.0 0.4 pad_maximum_fusion.1
  139.3 0.9 fusion.33
  140.3 0.9 fusion.49
  141.4 0.9 convolution_add_fusion.1
  142.4 0.9 fusion.9
  143.3 0.2 copy.20
  143.5 1.3 reshape.221
  (33 shorter events, 0.6 us)
Async XLA Ops:
  6.5 50.4 %copy-start = (bf16[384,384]{1,0:T(8,128)(2,1)S(1)}, bf16[384,384]{1,0:T(8,128)(2,1)}, u32[]{:S(2)}) copy-start(bf16[384,384]{1,0:T(8,128)(2,1)} %param.12) | copy-start | bytes 884740
  6.5 50.4 %all-gather.3.cloned.1.call-start = ((), (), s32[]{:S(2)}) async-start(), calls=%async_computation | async-start | bytes 3342336 | tf_op jit(solution)/shard_map/all_gather | solution.py:77
  10.6 92.4 %all-gather.5.cloned.1.call-start = ((), (), s32[]{:S(2)}) async-start(), calls=%async_computation.1 | async-start | bytes 3342336 | tf_op jit(solution)/shard_map/all_gather | solution.py:78
  62.2 40.8 %copy-start.7 = (bf16[1,2,128,384]{3,2,1,0:T(8,128)(2,1)S(1)}, bf16[1,2,128,384]{3,2,1,0:T(8,128)(2,1)}, u32[]{:S(2)}) copy-start(bf16[1,2,128,384]{3,2,1,0:T(8,128)(2,1)} %param.10) | copy-start | bytes 589828
  62.2 40.8 %copy-start.9 = (bf16[384,384]{1,0:T(8,128)(2,1)S(1)}, bf16[384,384]{1,0:T(8,128)(2,1)}, u32[]{:S(2)}) copy-start(bf16[384,384]{1,0:T(8,128)(2,1)} %param.15) | copy-start | bytes 884740
  103.0 4.8 %copy-start.8 = (f32[384]{0:T(512)S(1)}, f32[384]{0:T(512)}, u32[]{:S(2)}) copy-start(f32[384]{0:T(512)} %param.17) | copy-start | bytes 4612
  103.0 5.0 %copy-start.2 = (bf16[2,2,128,384]{3,2,1,0:T(8,128)(2,1)S(1)}, bf16[2,2,128,384]{3,2,1,0:T(8,128)(2,1)}, u32[]{:S(2)}) copy-start(bf16[2,2,128,384]{3,2,1,0:T(8,128)(2,1)} %param.16) | copy-start | bytes 1179652
  108.2 10.0 %collective-permute-start = (bf16[3,1,128,384]{3,2,1,0:T(8,128)(2,1)S(1)}, bf16[3,1,128,384]{3,2,1,0:T(8,128)(2,1)S(1)}, u32[]{:S(2)}, u32[]{:S(2)}) collective-permute-start(bf16[3,1,128,384]{3,2,1,0:T(8,128)(2,1)S(1)} %get-tuple-element.33), channel_id=1, source_target_pairs={{0,1},{1,2},{2,3},{3,4},{4,5},{5,6},{6,7},{7,8},{8,9},{9,10},{10,1... | collective-permute-start | bytes 884744 | tf_op jit(solution)/shard_map/ppermute | solution.py:16
  112.3 8.9 %collective-permute-start.1 = (bf16[3,1,128,384]{3,2,1,0:T(8,128)(2,1)S(1)}, bf16[3,1,128,384]{3,2,1,0:T(8,128)(2,1)S(1)}, u32[]{:S(2)}, u32[]{:S(2)}) collective-permute-start(bf16[3,1,128,384]{3,2,1,0:T(8,128)(2,1)S(1)} %get-tuple-element.34), channel_id=1, source_target_pairs={{1,0},{2,1},{3,2},{4,3},{5,4},{6,5},{7,6},{8,7},{9,8},{10,9},{11,1... | collective-permute-start | bytes 884744 | tf_op jit(solution)/shard_map/ppermute | solution.py:17
  127.2 5.2 %copy-start.6 = (bf16[3,3,384,192]{2,3,1,0:T(8,128)(2,1)S(1)}, bf16[3,3,384,192]{2,3,1,0:T(8,128)(2,1)}, u32[]{:S(2)}) copy-start(bf16[3,3,384,192]{2,3,1,0:T(8,128)(2,1)} %param.19) | copy-start | bytes 3981316
  127.9 8.3 %collective-permute-start.2 = (bf16[1,1,128,384]{3,2,1,0:T(8,128)(2,1)S(1)}, bf16[1,1,128,384]{3,2,1,0:T(8,128)(2,1)S(1)}, u32[]{:S(2)}, u32[]{:S(2)}) collective-permute-start(bf16[1,1,128,384]{3,2,1,0:T(8,128)(2,1)S(1)} %get-tuple-element.35), channel_id=1, source_target_pairs={{0,1},{1,2},{2,3},{3,4},{4,5},{5,6},{6,7},{7,8},{8,9},{9,10},{10,1... | collective-permute-start | bytes 294920 | tf_op jit(solution)/shard_map/ppermute | solution.py:16
  129.9 6.8 %collective-permute-start.3 = (bf16[1,1,128,384]{3,2,1,0:T(8,128)(2,1)S(1)}, bf16[1,1,128,384]{3,2,1,0:T(8,128)(2,1)S(1)}, u32[]{:S(2)}, u32[]{:S(2)}) collective-permute-start(bf16[1,1,128,384]{3,2,1,0:T(8,128)(2,1)S(1)} %get-tuple-element.36), channel_id=1, source_target_pairs={{1,0},{2,1},{3,2},{4,3},{5,4},{6,5},{7,6},{8,7},{9,8},{10,9},{11,1... | collective-permute-start | bytes 294920 | tf_op jit(solution)/shard_map/ppermute | solution.py:17
  139.3 1.0 copy-start.4
  140.3 1.0 copy-start.3
  141.4 1.0 copy-start.5
  142.4 2.5 %copy-start.1 = (bf16[384,384]{1,0:T(8,128)(2,1)S(1)}, bf16[384,384]{1,0:T(8,128)(2,1)}, u32[]{:S(2)}) copy-start(bf16[384,384]{1,0:T(8,128)(2,1)} %param.12) | copy-start | bytes 884740
Sparse Core Ops, SparseCore 0:
  10.8 46.1 all-gather.2
  59.2 43.7 all-gather.4
where the time goes:
time: 152 us
  waiting for transfers between devices  85.7 us (56%)
  matrix products  21.2 us (14%)
  local copies, waits for them, and re-layouts  13.9 us (9%)
  between operations  13.7 us (9%)
  starting transfers between devices  10.6 us (7%)
  other arithmetic  6.63 us (4%)
    all_gather x1, waiting for transfers between devices, body(): lax.all_gather(keys, 'rows', axis=1, tiled=True).reshape(nframes, -1, chans)  44.3 us
    all_gather x1, waiting for transfers between devices, body(): lax.all_gather(values, 'rows', axis=1, tiled=True)  37.8 us
    dot_general x12, matrix products, conv_core(): jnp.dot(part, weight[tstep, rstep].reshape(3 * chans, outs), preferred_el...  7.22 us
    ppermute x2, starting transfers between devices, padded_2(): before = lax.ppermute(last, axis, up)  6.06 us
    dot_general x1, matrix products, attend_block(): jnp.einsum('fqc,fkc->fqk', queries, keys, preferred_element_type=jnp.floa...  5.32 us
    slice x5, local copies, waits for them, and re-layouts, conv_core(): weight[tstep, rstep].reshape(3 * chans, outs)  5.2 us
    dot_general x1, matrix products, body(): jnp.einsum('fqc,cd->fqd', attended, w_out, preferred_element_type=jnp.flo...  4.82 us
    ppermute x2, starting transfers between devices, padded_2(): after = lax.ppermute(first, axis, down)  4.51 us
  transfers between devices with their start and end apart: 6, of which 4 were waited for; matrix products, arithmetic and copies ran while one was open for 12% of the time, Pallas kernels for 0%

commit v1 on v0

--- a/solution.py
+++ b/solution.py
@@ -1,9 +1,40 @@
+import functools
 import jax
 import jax.numpy as jnp
 from jax import lax
 from jax.sharding import PartitionSpec as P
 
 EPS = 1e-06
+
+
+def detail_yards(arr_in, a_name):
+    vec_out = jax.lax.axis_index(a_name)
+    local_now = jax.lax.axis_size(a_name)
+    by_rank = []
+    item_now, shaped, s_next = (local_now, vec_out, arr_in.shape[1])
+    for s in range(item_now):
+        by_rank.append((s, (s + 1) % item_now))
+    blocks_here = []
+    for s in range(item_now):
+        blocks_here.append((s, (s - 1) % item_now))
+    arr_next = jnp.zeros((*arr_in.shape[:1], item_now * s_next, *arr_in.shape[2:]), arr_in.dtype)
+    arr_next = lax.dynamic_update_slice_in_dim(arr_next, arr_in, shaped * s_next, axis=1)
+    oldest = item_now // 2
+    right_arr = passed = arr_in
+    for c in range(1, oldest + 1):
+        right_arr = jax.lax.ppermute(right_arr, a_name, by_rank)
+        arr_next = lax.dynamic_update_slice_in_dim(
+            arr_next, right_arr, (shaped - c) % item_now * s_next, axis=1
+        )
+        if c < item_now - oldest:
+            passed = jax.lax.ppermute(passed, a_name, blocks_here)
+            arr_next = lax.dynamic_update_slice_in_dim(
+                arr_next, passed, (shaped + c) % item_now * s_next, axis=1
+            )
+    return arr_next
+
+
+track_quarters = functools.partial(detail_yards, a_name="rows")
 
 
 def padded_2(array, sides, width):
@@ -75,7 +106,7 @@
     keys = project(normed, w_key).reshape(nframes, nrows, ncols, chans)
     values = project(normed, w_value).reshape(nframes, nrows, ncols, chans)
     keys_in = lax.all_gather(keys, "rows", axis=1, tiled=True).reshape(nframes, -1, chans)
-    values_in = lax.all_gather(values, "rows", axis=1, tiled=True).reshape(nframes, -1, chans)
+    values_in = track_quarters(values).reshape(nframes, -1, chans)
     carry = attend_block(start_carry, queries, keys_in, values_in, scale)
     attended = (carry[2] / carry[1][..., None]).astype(jnp.bfloat16)
     mixed = (

time: 152 us -> 138 us (0.908)
  the two profiles are of different devices: /device:TPU:5 before, /device:TPU:1 now
where the time goes in v1:
time: 138 us
  starting transfers between devices  57.8 us (42%)
  matrix products  22.4 us (16%)
  waiting for transfers between devices  19.6 us (14%)
  local copies, waits for them, and re-layouts  17.6 us (13%)
  between operations  13.9 us (10%)
  other arithmetic  6.62 us (5%)
    ppermute x7, starting transfers between devices, detail_yards(): passed = jax.lax.ppermute(passed, a_name, blocks_here)  35.1 us
    ppermute x8, waiting for transfers between devices, detail_yards(): right_arr = jax.lax.ppermute(right_arr, a_name, by_rank)  14.1 us
    ppermute x2, starting transfers between devices, padded_2(): after = lax.ppermute(first, axis, down)  11 us
    ppermute x8, starting transfers between devices, detail_yards(): right_arr = jax.lax.ppermute(right_arr, a_name, by_rank)  7.85 us
    dot_general x12, matrix products, conv_core(): jnp.dot(part, weight[tstep, rstep].reshape(3 * chans, outs), preferred_el...  7.17 us
    dot_general x1, matrix products, attend_block(): jnp.einsum('fqc,fkc->fqk', queries, keys, preferred_element_type=jnp.floa...  6.52 us
    ppermute x7, waiting for transfers between devices, detail_yards(): passed = jax.lax.ppermute(passed, a_name, blocks_here)  5.49 us
    slice x5, local copies, waits for them, and re-layouts, conv_core(): weight[tstep, rstep].reshape(3 * chans, outs)  5.2 us
  transfers between devices with their start and end apart: 20, of which 13 were waited for; matrix products, arithmetic and copies ran while one was open for 10% of the time, Pallas kernels for 0%

profile of v1, /device:TPU:1, one launch (start us, length us, event | category | flops | bytes accessed | tf_op | source)
XLA Modules:
  0.0 137.9 jit_solution(13766560684372826078)
XLA Ops:
  6.5 1.1 multiply_reduce_fusion.1
  7.6 1.0 fusion.29
  8.7 2.0 %convolution_convert_fusion.1 = bf16[256,384]{1,0:T(8,128)(2,1)} fusion(bf16[256,384]{1,0:T(8,128)(2,1)S(1)} %fusion.29, bf16[384,384]{1,0:T(8,128)(2,1)} %param.13), kind=kOutput, calls=%fused_computation.30 | convolution fusion | flops 75595776 | bytes 688128 | tf_op jit(solution)/shard_map/fqc,cd->fqd/dot_general | solution.py:58
  10.7 1.9 %convolution_convert_fusion = bf16[256,384]{1,0:T(8,128)(2,1)} fusion(bf16[256,384]{1,0:T(8,128)(2,1)S(1)} %fusion.29, bf16[384,384]{1,0:T(8,128)(2,1)} %param.14), kind=kOutput, calls=%fused_computation.29 | convolution fusion | flops 75595776 | bytes 688128 | tf_op jit(solution)/shard_map/fqc,cd->fqd/dot_general | solution.py:58
  12.6 2.6 %collective-permute-start = (bf16[1,2,128,384]{3,2,1,0:T(8,128)(2,1)}, bf16[1,2,128,384]{3,2,1,0:T(8,128)(2,1)}, u32[]{:S(2)}, u32[]{:S(2)}) collective-permute-start(bf16[1,2,128,384]{3,2,1,0:T(8,128)(2,1)} %bitcast.5), channel_id=1, source_target_pairs={{0,1},{1,2},{2,3},{3,4},{4,5},{5,6},{6,7},{7,8},{8,9},{9,10},{10,1... | collective-permute-start | bytes 589832 | tf_op jit(solution)/shard_map/ppermute | solution.py:25
  15.7 1.0 constant_dynamic-update-slice_fusion.15
  16.7 1.5 %collective-permute-done = bf16[1,2,128,384]{3,2,1,0:T(8,128)(2,1)} collective-permute-done((bf16[1,2,128,384]{3,2,1,0:T(8,128)(2,1)}, bf16[1,2,128,384]{3,2,1,0:T(8,128)(2,1)}, u32[]{:S(2)}, u32[]{:S(2)}) %collective-permute-start) | collective-permute-done | bytes 196640 | tf_op jit(solution)/shard_map/ppermute | solution.py:25
  18.2 2.5 %collective-permute-start.2 = (bf16[1,2,128,384]{3,2,1,0:T(8,128)(2,1)}, bf16[1,2,128,384]{3,2,1,0:T(8,128)(2,1)S(1)}, u32[]{:S(2)}, u32[]{:S(2)}) collective-permute-start(bf16[1,2,128,384]{3,2,1,0:T(8,128)(2,1)} %collective-permute-done), channel_id=1, source_target_pairs={{0,1},{1,2},{2,3},{3,4},{4,5},{5,6},{6,7},{7,8},{8,9},{9,10},{10,1... | collective-permute-start | bytes 589832 | tf_op jit(solution)/shard_map/ppermute | solution.py:25
  20.6 2.1 %collective-permute-done.1 = bf16[1,2,128,384]{3,2,1,0:T(8,128)(2,1)} collective-permute-done((bf16[1,2,128,384]{3,2,1,0:T(8,128)(2,1)}, bf16[1,2,128,384]{3,2,1,0:T(8,128)(2,1)}, u32[]{:S(2)}, u32[]{:S(2)}) %collective-permute-start.1) | collective-permute-done | bytes 196640 | tf_op jit(solution)/shard_map/ppermute | solution.py:30
  22.8 1.0 constant_dynamic-update-slice_fusion.14
  23.7 1.0 constant_dynamic-update-slice_fusion.13
  24.7 2.7 %collective-permute-done.2 = bf16[1,2,128,384]{3,2,1,0:T(8,128)(2,1)S(1)} collective-permute-done((bf16[1,2,128,384]{3,2,1,0:T(8,128)(2,1)}, bf16[1,2,128,384]{3,2,1,0:T(8,128)(2,1)S(1)}, u32[]{:S(2)}, u32[]{:S(2)}) %collective-permute-start.2) | collective-permute-done | bytes 196640 | tf_op jit(solution)/shard_map/ppermute | solution.py:25
  27.4 2.5 %collective-permute-start.4 = (bf16[1,2,128,384]{3,2,1,0:T(8,128)(2,1)S(1)}, bf16[1,2,128,384]{3,2,1,0:T(8,128)(2,1)S(1)}, u32[]{:S(2)}, u32[]{:S(2)}) collective-permute-start(bf16[1,2,128,384]{3,2,1,0:T(8,128)(2,1)S(1)} %collective-permute-done.2), channel_id=1, source_target_pairs={{0,1},{1,2},{2,3},{3,4},{4,5},{5,6},{6,7},{7,8},{8,9},{9,10},{10,1... | collective-permute-start | bytes 589832 | tf_op jit(solution)/shard_map/ppermute | solution.py:25
  29.9 4.0 %collective-permute-start.5 = (bf16[1,2,128,384]{3,2,1,0:T(8,128)(2,1)S(1)}, bf16[1,2,128,384]{3,2,1,0:T(8,128)(2,1)S(1)}, u32[]{:S(2)}, u32[]{:S(2)}) collective-permute-start(bf16[1,2,128,384]{3,2,1,0:T(8,128)(2,1)S(1)} %collective-permute-done.3), channel_id=1, source_target_pairs={{0,15},{1,0},{2,1},{3,2},{4,3},{5,4},{6,5},{7,6},{8,7},{9,8},{10,9... | collective-permute-start | bytes 589832 | tf_op jit(solution)/shard_map/ppermute | solution.py:30
  34.0 0.8 collective-permute-done.4
  35.0 0.5 collective-permute-done.5
  35.5 7.8 %collective-permute-start.7 = (bf16[1,2,128,384]{3,2,1,0:T(8,128)(2,1)S(1)}, bf16[1,2,128,384]{3,2,1,0:T(8,128)(2,1)S(1)}, u32[]{:S(2)}, u32[]{:S(2)}) collective-permute-start(bf16[1,2,128,384]{3,2,1,0:T(8,128)(2,1)S(1)} %collective-permute-done.5), channel_id=1, source_target_pairs={{0,15},{1,0},{2,1},{3,2},{4,3},{5,4},{6,5},{7,6},{8,7},{9,8},{10,9... | collective-permute-start | bytes 589832 | tf_op jit(solution)/shard_map/ppermute | solution.py:30
  43.5 0.9 collective-permute-done.7
  44.4 9.3 %collective-permute-start.9 = (bf16[1,2,128,384]{3,2,1,0:T(8,128)(2,1)S(1)}, bf16[1,2,128,384]{3,2,1,0:T(8,128)(2,1)S(1)}, u32[]{:S(2)}, u32[]{:S(2)}) collective-permute-start(bf16[1,2,128,384]{3,2,1,0:T(8,128)(2,1)S(1)} %collective-permute-done.7), channel_id=1, source_target_pairs={{0,15},{1,0},{2,1},{3,2},{4,3},{5,4},{6,5},{7,6},{8,7},{9,8},{10,9... | collective-permute-start | bytes 589832 | tf_op jit(solution)/shard_map/ppermute | solution.py:30
  53.8 0.8 collective-permute-done.8
  54.7 1.0 collective-permute-done.9
  55.7 7.1 %collective-permute-start.11 = (bf16[1,2,128,384]{3,2,1,0:T(8,128)(2,1)S(1)}, bf16[1,2,128,384]{3,2,1,0:T(8,128)(2,1)S(1)}, u32[]{:S(2)}, u32[]{:S(2)}) collective-permute-start(bf16[1,2,128,384]{3,2,1,0:T(8,128)(2,1)S(1)} %collective-permute-done.9), channel_id=1, source_target_pairs={{0,15},{1,0},{2,1},{3,2},{4,3},{5,4},{6,5},{7,6},{8,7},{9,8},{10,9... | collective-permute-start | bytes 589832 | tf_op jit(solution)/shard_map/ppermute | solution.py:30
  63.3 0.5 collective-permute-done.11
  63.8 6.8 %collective-permute-start.13 = (bf16[1,2,128,384]{3,2,1,0:T(8,128)(2,1)S(1)}, bf16[1,2,128,384]{3,2,1,0:T(8,128)(2,1)S(1)}, u32[]{:S(2)}, u32[]{:S(2)}) collective-permute-start(bf16[1,2,128,384]{3,2,1,0:T(8,128)(2,1)S(1)} %collective-permute-done.11), channel_id=1, source_target_pairs={{0,15},{1,0},{2,1},{3,2},{4,3},{5,4},{6,5},{7,6},{8,7},{9,8},{10,9... | collective-permute-start | bytes 589832 | tf_op jit(solution)/shard_map/ppermute | solution.py:30
  71.7 7.2 %collective-permute-done.14 = bf16[1,2,128,384]{3,2,1,0:T(8,128)(2,1)S(1)} collective-permute-done((bf16[1,2,128,384]{3,2,1,0:T(8,128)(2,1)S(1)}, bf16[1,2,128,384]{3,2,1,0:T(8,128)(2,1)S(1)}, u32[]{:S(2)}, u32[]{:S(2)}) %collective-permute-start.14) | collective-permute-done | bytes 196640 | tf_op jit(solution)/shard_map/ppermute | solution.py:25
  79.1 6.5 %fusion.38 = (f32[256]{0:T(256)S(1)}, f32[256,4096]{1,0:T(8,128)}) fusion(bf16[4096,384]{1,0:T(8,128)(2,1)} %bitcast.107, bf16[256,384]{1,0:T(8,128)(2,1)} %copy-done.4, bf16[384,384]{1,0:T(8,128)(2,1)S(1)} %copy-done), kind=kOutput, calls=%fused_computation.75 | convolution fusion | flops 882999040 | bytes 7832576 | tf_op jit(solution)/shard_map/fqc,fkc->fqk/dot_general | solution.py:83
  85.6 2.9 %fusion = f32[256]{0:T(256)S(1)} fusion(f32[256,4096]{1,0:T(8,128)} %get-tuple-element.38, f32[256]{0:T(256)S(1)} %broadcast_maximum_fusion), kind=kLoop, calls=%fused_computation.4 | loop fusion | flops 2096896 | bytes 4196352 | tf_op jit(solution)/shard_map/reduce_sum | solution.py:86
  88.6 4.8 %multiply_reduce_fusion = (f32[256]{0:T(256)S(1)}, f32[256,384]{1,0:T(8,128)S(1)}) fusion(bf16[384,384]{1,0:T(8,128)(2,1)S(1)} %copy-done.11, bf16[4096,384]{1,0:T(8,128)(2,1)} %bitcast.105, f32[256,4096]{1,0:T(8,128)} %get-tuple-element.38, f32[256]{0:T(256)S(1)} %broadcast_maximum_fusion, f32[256]{0:T(256)S(1)} %fusion, bf16[256,384]{1,0:T(8,128)(2,1)S(1)} %bitcast.126), kind=kOutput, calls=%fused_computation.45 | convolution fusion | flops 883687168 | bytes 8227840 | tf_op jit(solution)/shard_map/fqc,cd->fqd/dot_general | solution.py:114
  93.7 1.9 %collective-permute-start.15 = (bf16[3,1,128,384]{3,2,1,0:T(8,128)(2,1)S(1)}, bf16[3,1,128,384]{3,2,1,0:T(8,128)(2,1)S(1)}, u32[]{:S(2)}, u32[]{:S(2)}) collective-permute-start(bf16[3,1,128,384]{3,2,1,0:T(8,128)(2,1)S(1)} %get-tuple-element.33), channel_id=1, source_target_pairs={{0,1},{1,2},{2,3},{3,4},{4,5},{5,6},{6,7},{7,8},{8,9},{9,10},{10,1... | collective-permute-start | bytes 884744 | tf_op jit(solution)/shard_map/ppermute | solution.py:47
  95.7 8.3 %collective-permute-start.16 = (bf16[3,1,128,384]{3,2,1,0:T(8,128)(2,1)S(1)}, bf16[3,1,128,384]{3,2,1,0:T(8,128)(2,1)S(1)}, u32[]{:S(2)}, u32[]{:S(2)}) collective-permute-start(bf16[3,1,128,384]{3,2,1,0:T(8,128)(2,1)S(1)} %get-tuple-element.34), channel_id=1, source_target_pairs={{1,0},{2,1},{3,2},{4,3},{5,4},{6,5},{7,6},{8,7},{9,8},{10,9},{11,1... | collective-permute-start | bytes 884744 | tf_op jit(solution)/shard_map/ppermute | solution.py:48
  104.0 3.9 %fusion.32 = (bf16[1,1,3,384,384]{4,3,2,1,0:T(8,128)(2,1)S(1)}, bf16[1,1,3,384,384]{4,3,2,1,0:T(8,128)(2,1)S(1)}, bf16[1,1,3,384,384]{4,3,2,1,0:T(8,128)(2,1)S(1...) fusion(bf16[3,3,3,384,384]{4,3,2,1,0:T(8,128)(2,1)} %param.18), kind=kLoop, calls=%fused_computation.69 | loop fusion | bytes 15925248 | tf_op jit(solution)/shard_map/slice | solution.py:75
  108.3 0.5 fusion.36
  108.8 0.5 pad_maximum_fusion
  109.4 0.7 fusion.34
  113.9 0.6 fusion.17
  114.6 1.9 %collective-permute-start.17 = (bf16[1,1,128,384]{3,2,1,0:T(8,128)(2,1)S(1)}, bf16[1,1,128,384]{3,2,1,0:T(8,128)(2,1)S(1)}, u32[]{:S(2)}, u32[]{:S(2)}) collective-permute-start(bf16[1,1,128,384]{3,2,1,0:T(8,128)(2,1)S(1)} %get-tuple-element.35), channel_id=1, source_target_pairs={{0,1},{1,2},{2,3},{3,4},{4,5},{5,6},{6,7},{7,8},{8,9},{9,10},{10,1... | collective-permute-start | bytes 294920 | tf_op jit(solution)/shard_map/ppermute | solution.py:47
  116.5 2.6 %collective-permute-start.18 = (bf16[1,1,128,384]{3,2,1,0:T(8,128)(2,1)S(1)}, bf16[1,1,128,384]{3,2,1,0:T(8,128)(2,1)S(1)}, u32[]{:S(2)}, u32[]{:S(2)}) collective-permute-start(bf16[1,1,128,384]{3,2,1,0:T(8,128)(2,1)S(1)} %get-tuple-element.36), channel_id=1, source_target_pairs={{1,0},{2,1},{3,2},{4,3},{5,4},{6,5},{7,6},{8,7},{9,8},{10,9},{11,1... | collective-permute-start | bytes 294920 | tf_op jit(solution)/shard_map/ppermute | solution.py:48
  119.7 0.8 copy.20
  120.9 0.8 copy.21
  122.1 0.8 copy.22
  123.1 0.8 broadcast_in_dim.29
  123.9 0.6 broadcast_in_dim.30
  124.7 0.5 pad_slice_fusion.1
  125.6 0.9 fusion.33
  126.6 0.9 fusion.49
  127.6 0.9 convolution_add_fusion.1
  128.6 0.9 fusion.9
  129.7 1.3 reshape.221
  (81 shorter events, 9.3 us)
Async XLA Ops:
  6.5 72.5 %copy-start = (bf16[384,384]{1,0:T(8,128)(2,1)S(1)}, bf16[384,384]{1,0:T(8,128)(2,1)}, u32[]{:S(2)}) copy-start(bf16[384,384]{1,0:T(8,128)(2,1)} %param.12) | copy-start | bytes 884740
  6.5 72.5 %all-gather.2.cloned.1.call-start = ((), (), s32[]{:S(2)}) async-start(), calls=%async_computation | async-start | bytes 3342336 | tf_op jit(solution)/shard_map/all_gather | solution.py:108
  8.7 6.5 %copy-start.4 = (bf16[256,384]{1,0:T(8,128)(2,1)}, bf16[256,384]{1,0:T(8,128)(2,1)S(1)}, u32[]{:S(2)}) copy-start(bf16[256,384]{1,0:T(8,128)(2,1)S(1)} %fusion.29) | copy-start | bytes 589828
  12.6 5.5 %collective-permute-start = (bf16[1,2,128,384]{3,2,1,0:T(8,128)(2,1)}, bf16[1,2,128,384]{3,2,1,0:T(8,128)(2,1)}, u32[]{:S(2)}, u32[]{:S(2)}) collective-permute-start(bf16[1,2,128,384]{3,2,1,0:T(8,128)(2,1)} %bitcast.5), channel_id=1, source_target_pairs={{0,1},{1,2},{2,3},{3,4},{4,5},{5,6},{6,7},{7,8},{8,9},{9,10},{10,1... | collective-permute-start | bytes 589832 | tf_op jit(solution)/shard_map/ppermute | solution.py:25
  15.2 7.5 %collective-permute-start.1 = (bf16[1,2,128,384]{3,2,1,0:T(8,128)(2,1)}, bf16[1,2,128,384]{3,2,1,0:T(8,128)(2,1)}, u32[]{:S(2)}, u32[]{:S(2)}) collective-permute-start(bf16[1,2,128,384]{3,2,1,0:T(8,128)(2,1)} %bitcast.5), channel_id=1, source_target_pairs={{0,15},{1,0},{2,1},{3,2},{4,3},{5,4},{6,5},{7,6},{8,7},{9,8},{10,9... | collective-permute-start | bytes 589832 | tf_op jit(solution)/shard_map/ppermute | solution.py:30
  18.2 9.2 %collective-permute-start.2 = (bf16[1,2,128,384]{3,2,1,0:T(8,128)(2,1)}, bf16[1,2,128,384]{3,2,1,0:T(8,128)(2,1)S(1)}, u32[]{:S(2)}, u32[]{:S(2)}) collective-permute-start(bf16[1,2,128,384]{3,2,1,0:T(8,128)(2,1)} %collective-permute-done), channel_id=1, source_target_pairs={{0,1},{1,2},{2,3},{3,4},{4,5},{5,6},{6,7},{7,8},{8,9},{9,10},{10,1... | collective-permute-start | bytes 589832 | tf_op jit(solution)/shard_map/ppermute | solution.py:25
  22.8 7.1 %collective-permute-start.3 = (bf16[1,2,128,384]{3,2,1,0:T(8,128)(2,1)}, bf16[1,2,128,384]{3,2,1,0:T(8,128)(2,1)S(1)}, u32[]{:S(2)}, u32[]{:S(2)}) collective-permute-start(bf16[1,2,128,384]{3,2,1,0:T(8,128)(2,1)} %collective-permute-done.1), channel_id=1, source_target_pairs={{0,15},{1,0},{2,1},{3,2},{4,3},{5,4},{6,5},{7,6},{8,7},{9,8},{10,9... | collective-permute-start | bytes 589832 | tf_op jit(solution)/shard_map/ppermute | solution.py:30
  27.4 7.4 %collective-permute-start.4 = (bf16[1,2,128,384]{3,2,1,0:T(8,128)(2,1)S(1)}, bf16[1,2,128,384]{3,2,1,0:T(8,128)(2,1)S(1)}, u32[]{:S(2)}, u32[]{:S(2)}) collective-permute-start(bf16[1,2,128,384]{3,2,1,0:T(8,128)(2,1)S(1)} %collective-permute-done.2), channel_id=1, source_target_pairs={{0,1},{1,2},{2,3},{3,4},{4,5},{5,6},{6,7},{7,8},{8,9},{9,10},{10,1... | collective-permute-start | bytes 589832 | tf_op jit(solution)/shard_map/ppermute | solution.py:25
  29.9 5.6 %collective-permute-start.5 = (bf16[1,2,128,384]{3,2,1,0:T(8,128)(2,1)S(1)}, bf16[1,2,128,384]{3,2,1,0:T(8,128)(2,1)S(1)}, u32[]{:S(2)}, u32[]{:S(2)}) collective-permute-start(bf16[1,2,128,384]{3,2,1,0:T(8,128)(2,1)S(1)} %collective-permute-done.3), channel_id=1, source_target_pairs={{0,15},{1,0},{2,1},{3,2},{4,3},{5,4},{6,5},{7,6},{8,7},{9,8},{10,9... | collective-permute-start | bytes 589832 | tf_op jit(solution)/shard_map/ppermute | solution.py:30
  34.8 8.6 %collective-permute-start.6 = (bf16[1,2,128,384]{3,2,1,0:T(8,128)(2,1)S(1)}, bf16[1,2,128,384]{3,2,1,0:T(8,128)(2,1)S(1)}, u32[]{:S(2)}, u32[]{:S(2)}) collective-permute-start(bf16[1,2,128,384]{3,2,1,0:T(8,128)(2,1)S(1)} %collective-permute-done.4), channel_id=1, source_target_pairs={{0,1},{1,2},{2,3},{3,4},{4,5},{5,6},{6,7},{7,8},{8,9},{9,10},{10,1... | collective-permute-start | bytes 589832 | tf_op jit(solution)/shard_map/ppermute | solution.py:25
  35.5 8.9 %collective-permute-start.7 = (bf16[1,2,128,384]{3,2,1,0:T(8,128)(2,1)S(1)}, bf16[1,2,128,384]{3,2,1,0:T(8,128)(2,1)S(1)}, u32[]{:S(2)}, u32[]{:S(2)}) collective-permute-start(bf16[1,2,128,384]{3,2,1,0:T(8,128)(2,1)S(1)} %collective-permute-done.5), channel_id=1, source_target_pairs={{0,15},{1,0},{2,1},{3,2},{4,3},{5,4},{6,5},{7,6},{8,7},{9,8},{10,9... | collective-permute-start | bytes 589832 | tf_op jit(solution)/shard_map/ppermute | solution.py:30
  43.4 11.2 %collective-permute-start.8 = (bf16[1,2,128,384]{3,2,1,0:T(8,128)(2,1)S(1)}, bf16[1,2,128,384]{3,2,1,0:T(8,128)(2,1)S(1)}, u32[]{:S(2)}, u32[]{:S(2)}) collective-permute-start(bf16[1,2,128,384]{3,2,1,0:T(8,128)(2,1)S(1)} %collective-permute-done.6), channel_id=1, source_target_pairs={{0,1},{1,2},{2,3},{3,4},{4,5},{5,6},{6,7},{7,8},{8,9},{9,10},{10,1... | collective-permute-start | bytes 589832 | tf_op jit(solution)/shard_map/ppermute | solution.py:25
  44.4 11.3 %collective-permute-start.9 = (bf16[1,2,128,384]{3,2,1,0:T(8,128)(2,1)S(1)}, bf16[1,2,128,384]{3,2,1,0:T(8,128)(2,1)S(1)}, u32[]{:S(2)}, u32[]{:S(2)}) collective-permute-start(bf16[1,2,128,384]{3,2,1,0:T(8,128)(2,1)S(1)} %collective-permute-done.7), channel_id=1, source_target_pairs={{0,15},{1,0},{2,1},{3,2},{4,3},{5,4},{6,5},{7,6},{8,7},{9,8},{10,9... | collective-permute-start | bytes 589832 | tf_op jit(solution)/shard_map/ppermute | solution.py:30
  54.7 8.6 %collective-permute-start.10 = (bf16[1,2,128,384]{3,2,1,0:T(8,128)(2,1)S(1)}, bf16[1,2,128,384]{3,2,1,0:T(8,128)(2,1)S(1)}, u32[]{:S(2)}, u32[]{:S(2)}) collective-permute-start(bf16[1,2,128,384]{3,2,1,0:T(8,128)(2,1)S(1)} %collective-permute-done.8), channel_id=1, source_target_pairs={{0,1},{1,2},{2,3},{3,4},{4,5},{5,6},{6,7},{7,8},{8,9},{9,10},{10,1... | collective-permute-start | bytes 589832 | tf_op jit(solution)/shard_map/ppermute | solution.py:25
  55.7 8.2 %collective-permute-start.11 = (bf16[1,2,128,384]{3,2,1,0:T(8,128)(2,1)S(1)}, bf16[1,2,128,384]{3,2,1,0:T(8,128)(2,1)S(1)}, u32[]{:S(2)}, u32[]{:S(2)}) collective-permute-start(bf16[1,2,128,384]{3,2,1,0:T(8,128)(2,1)S(1)} %collective-permute-done.9), channel_id=1, source_target_pairs={{0,15},{1,0},{2,1},{3,2},{4,3},{5,4},{6,5},{7,6},{8,7},{9,8},{10,9... | collective-permute-start | bytes 589832 | tf_op jit(solution)/shard_map/ppermute | solution.py:30
  63.3 7.9 %collective-permute-start.12 = (bf16[1,2,128,384]{3,2,1,0:T(8,128)(2,1)S(1)}, bf16[1,2,128,384]{3,2,1,0:T(8,128)(2,1)S(1)}, u32[]{:S(2)}, u32[]{:S(2)}) collective-permute-start(bf16[1,2,128,384]{3,2,1,0:T(8,128)(2,1)S(1)} %collective-permute-done.10), channel_id=1, source_target_pairs={{0,1},{1,2},{2,3},{3,4},{4,5},{5,6},{6,7},{7,8},{8,9},{9,10},{10,1... | collective-permute-start | bytes 589832 | tf_op jit(solution)/shard_map/ppermute | solution.py:25
  63.8 7.9 %collective-permute-start.13 = (bf16[1,2,128,384]{3,2,1,0:T(8,128)(2,1)S(1)}, bf16[1,2,128,384]{3,2,1,0:T(8,128)(2,1)S(1)}, u32[]{:S(2)}, u32[]{:S(2)}) collective-permute-start(bf16[1,2,128,384]{3,2,1,0:T(8,128)(2,1)S(1)} %collective-permute-done.11), channel_id=1, source_target_pairs={{0,15},{1,0},{2,1},{3,2},{4,3},{5,4},{6,5},{7,6},{8,7},{9,8},{10,9... | collective-permute-start | bytes 589832 | tf_op jit(solution)/shard_map/ppermute | solution.py:30
  71.2 7.8 %collective-permute-start.14 = (bf16[1,2,128,384]{3,2,1,0:T(8,128)(2,1)S(1)}, bf16[1,2,128,384]{3,2,1,0:T(8,128)(2,1)S(1)}, u32[]{:S(2)}, u32[]{:S(2)}) collective-permute-start(bf16[1,2,128,384]{3,2,1,0:T(8,128)(2,1)S(1)} %collective-permute-done.12), channel_id=1, source_target_pairs={{0,1},{1,2},{2,3},{3,4},{4,5},{5,6},{6,7},{7,8},{8,9},{9,10},{10,1... | collective-permute-start | bytes 589832 | tf_op jit(solution)/shard_map/ppermute | solution.py:25
  79.0 6.6 %copy-start.3 = (bf16[1,32,128,384]{3,2,1,0:T(8,128)(2,1)}, bf16[1,32,128,384]{3,2,1,0:T(8,128)(2,1)S(1)}, u32[]{:S(2)}) copy-start(bf16[1,32,128,384]{3,2,1,0:T(8,128)(2,1)S(1)} %constant_dynamic-update-slice_fusion) | copy-start | bytes 9437188
  85.6 3.0 %copy-start.9 = (bf16[1,2,128,384]{3,2,1,0:T(8,128)(2,1)S(1)}, bf16[1,2,128,384]{3,2,1,0:T(8,128)(2,1)}, u32[]{:S(2)}) copy-start(bf16[1,2,128,384]{3,2,1,0:T(8,128)(2,1)} %param.10) | copy-start | bytes 589828
  85.6 3.0 %copy-start.11 = (bf16[384,384]{1,0:T(8,128)(2,1)S(1)}, bf16[384,384]{1,0:T(8,128)(2,1)}, u32[]{:S(2)}) copy-start(bf16[384,384]{1,0:T(8,128)(2,1)} %param.15) | copy-start | bytes 884740
  88.6 4.9 %copy-start.10 = (f32[384]{0:T(512)S(1)}, f32[384]{0:T(512)}, u32[]{:S(2)}) copy-start(f32[384]{0:T(512)} %param.17) | copy-start | bytes 4612
  88.6 5.0 %copy-start.2 = (bf16[2,2,128,384]{3,2,1,0:T(8,128)(2,1)S(1)}, bf16[2,2,128,384]{3,2,1,0:T(8,128)(2,1)}, u32[]{:S(2)}) copy-start(bf16[2,2,128,384]{3,2,1,0:T(8,128)(2,1)} %param.16) | copy-start | bytes 1179652
  93.7 14.2 %collective-permute-start.15 = (bf16[3,1,128,384]{3,2,1,0:T(8,128)(2,1)S(1)}, bf16[3,1,128,384]{3,2,1,0:T(8,128)(2,1)S(1)}, u32[]{:S(2)}, u32[]{:S(2)}) collective-permute-start(bf16[3,1,128,384]{3,2,1,0:T(8,128)(2,1)S(1)} %get-tuple-element.33), channel_id=1, source_target_pairs={{0,1},{1,2},{2,3},{3,4},{4,5},{5,6},{6,7},{7,8},{8,9},{9,10},{10,1... | collective-permute-start | bytes 884744 | tf_op jit(solution)/shard_map/ppermute | solution.py:47
  95.7 12.3 %collective-permute-start.16 = (bf16[3,1,128,384]{3,2,1,0:T(8,128)(2,1)S(1)}, bf16[3,1,128,384]{3,2,1,0:T(8,128)(2,1)S(1)}, u32[]{:S(2)}, u32[]{:S(2)}) collective-permute-start(bf16[3,1,128,384]{3,2,1,0:T(8,128)(2,1)S(1)} %get-tuple-element.34), channel_id=1, source_target_pairs={{1,0},{2,1},{3,2},{4,3},{5,4},{6,5},{7,6},{8,7},{9,8},{10,9},{11,1... | collective-permute-start | bytes 884744 | tf_op jit(solution)/shard_map/ppermute | solution.py:48
  113.4 5.7 %copy-start.8 = (bf16[3,3,384,192]{2,3,1,0:T(8,128)(2,1)S(1)}, bf16[3,3,384,192]{2,3,1,0:T(8,128)(2,1)}, u32[]{:S(2)}) copy-start(bf16[3,3,384,192]{2,3,1,0:T(8,128)(2,1)} %param.19) | copy-start | bytes 3981316
  114.6 8.4 %collective-permute-start.17 = (bf16[1,1,128,384]{3,2,1,0:T(8,128)(2,1)S(1)}, bf16[1,1,128,384]{3,2,1,0:T(8,128)(2,1)S(1)}, u32[]{:S(2)}, u32[]{:S(2)}) collective-permute-start(bf16[1,1,128,384]{3,2,1,0:T(8,128)(2,1)S(1)} %get-tuple-element.35), channel_id=1, source_target_pairs={{0,1},{1,2},{2,3},{3,4},{4,5},{5,6},{6,7},{7,8},{8,9},{9,10},{10,1... | collective-permute-start | bytes 294920 | tf_op jit(solution)/shard_map/ppermute | solution.py:47
  116.5 6.5 %collective-permute-start.18 = (bf16[1,1,128,384]{3,2,1,0:T(8,128)(2,1)S(1)}, bf16[1,1,128,384]{3,2,1,0:T(8,128)(2,1)S(1)}, u32[]{:S(2)}, u32[]{:S(2)}) collective-permute-start(bf16[1,1,128,384]{3,2,1,0:T(8,128)(2,1)S(1)} %get-tuple-element.36), channel_id=1, source_target_pairs={{1,0},{2,1},{3,2},{4,3},{5,4},{6,5},{7,6},{8,7},{9,8},{10,9},{11,1... | collective-permute-start | bytes 294920 | tf_op jit(solution)/shard_map/ppermute | solution.py:48
  125.6 1.0 copy-start.6
  126.5 1.0 copy-start.5
  127.6 1.0 copy-start.7
  128.5 2.6 %copy-start.1 = (bf16[384,384]{1,0:T(8,128)(2,1)S(1)}, bf16[384,384]{1,0:T(8,128)(2,1)}, u32[]{:S(2)}) copy-start(bf16[384,384]{1,0:T(8,128)(2,1)} %param.12) | copy-start | bytes 884740
Sparse Core Ops, SparseCore 0:
  10.8 56.4 all-gather.1
